TPU v7x, 512 devices: a whole 4x8x8 slice. The times are simulated.
512 devices in a mesh: seq: 32 (over x, y), head: 8 (over z), doc: 2 (over core).
Axes of the slice: x: 4, y: 8, z: 8, core: 2. Of those that a mesh axis runs over, the one named last changes fastest.
Arguments:
- byte_states: bfloat16 [32768, 1024], P(('doc', 'seq')), parts along dimension 0, may hold values from -36 to 36
- conv_kernel: float32 [4, 1024], replicated, may hold values from -3 to 3
- mix_weight: bfloat16 [1024, 1024], replicated, may hold values from -0.1875 to 0.1875
- norm_gain: float32 [1024], replicated, may hold values from 0.1 to 1.9
- query_weight: bfloat16 [1024, 1024], P(None, 'head'), may hold values from -3 to 3
- key_weight: bfloat16 [1024, 1024], P(None, 'head'), may hold values from -3 to 3
- value_weight: bfloat16 [1024, 1024], P(None, 'head'), may hold values from -0.1875 to 0.1875
- boundaries: int32 [4096], P(('doc', 'seq')), parts along dimension 0, may hold values from 0 to 511, as said below
- span_counts: int32 [64], P(('doc', 'seq')), parts along dimension 0, may hold values from 16 to 64, as said below
- grad_attended: bfloat16 [4096, 1024], P(('doc', 'seq'), 'head'), parts along dimension 0, may hold values from -6 to 6
Outputs:
- attended: bfloat16 [4096, 1024], P(('doc', 'seq'), 'head'), parts along dimension 0
- grad_bytes: bfloat16 [32768, 1024], P(('doc', 'seq')), parts along dimension 0
There are 2 independent parts, one for each index of `doc`. A program takes and returns all parts, laid end to end along the dimension named above; an argument that names none is the same for every part. Nothing has to cross between parts.
Inputs may be any that keep to these rules, and one draw needn't show every extreme that they name: `span_counts`: number of spans starting in each shard; in every draw some shard has exactly 64. `boundaries`: in each shard's 64 slots the first span_counts entries are strictly increasing byte positions inside the shard, the first of them 0; the remaining slots hold 0.
All inputs are finite; a program needn't handle non-finite values.
Results may differ from a plain program's by a relative error of at most 0.017.
Values may be sent and summed in bfloat16 or wider, within the bound.
No kernel may reach another device: no remote copies, remote signals or barrier semaphores. Data moves between devices by JAX's collectives and lax.ppermute only.
A program may use at most 64 MiB of HBM per device.

v0:
```python
import math
import jax
import jax.numpy as jnp
from jax import lax
from jax.sharding import PartitionSpec as P

D = 1024
HD = 128
KCONV = 4
masked_score = -1e30


def passed_along(array, axis, by):
    devices = lax.axis_size(axis)
    pairs = [(i, i + by) for i in range(devices) if 0 <= i + by < devices]
    return lax.ppermute(array, axis, pairs)


def neighbour(rim_rows, offset_by):
    return passed_along(rim_rows, "seq", offset_by)


def per_device(
    byte_states,
    conv_kernel,
    mix_weight,
    norm_gain,
    query_weight,
    key_weight,
    value_weight,
    boundaries,
    span_counts,
    grad_attended,
):
    row_count = byte_states.shape[0]
    slot_count = boundaries.shape[0]
    head_width = query_weight.shape[1]
    local_heads = head_width // HD
    score_scale = 1.0 / math.sqrt(HD)
    shard_index = lax.axis_index("seq")
    first_slot = shard_index * slot_count
    own_ids = first_slot + jnp.arange(slot_count, dtype=jnp.int32)
    before_rim = neighbour(byte_states[row_count - (KCONV - 1) :].astype(jnp.float32), 1)
    extended = jnp.concatenate([before_rim.astype(jnp.bfloat16), byte_states], axis=0)
    span_depth = conv_kernel[0] * jnp.take(extended, boundaries + (KCONV - 1), axis=0).astype(
        jnp.float32
    )
    for offset in range(1, KCONV):
        tapped = jnp.take(extended, boundaries + (KCONV - 1 - offset), axis=0).astype(jnp.float32)
        span_depth = span_depth + conv_kernel[offset] * tapped
    span_depth = span_depth.astype(jnp.bfloat16)
    span_bytes = jnp.take(byte_states, boundaries, axis=0).astype(jnp.float32)
    live_mask = jnp.arange(slot_count, dtype=jnp.int32) < span_counts[0]
    live_half = live_mask.astype(jnp.bfloat16)
    span_state = span_bytes + jnp.dot(span_depth, mix_weight, preferred_element_type=jnp.float32)
    inverse_rms = lax.rsqrt(jnp.mean(span_state * span_state, axis=1) + 1e-05)
    normed = (span_state * inverse_rms[:, None] * norm_gain).astype(jnp.bfloat16)
    queries = jnp.dot(normed, query_weight, preferred_element_type=jnp.float32).astype(jnp.bfloat16)
    key_rows = jnp.dot(normed, key_weight, preferred_element_type=jnp.float32).astype(jnp.bfloat16)
    value_rows = jnp.dot(normed, value_weight, preferred_element_type=jnp.float32).astype(
        jnp.bfloat16
    )
    grad_rows = jnp.where(live_mask[:, None], grad_attended, jnp.zeros_like(grad_attended))
    query_heads = queries.reshape(slot_count, local_heads, HD)
    key_heads = key_rows.reshape(slot_count, local_heads, HD)
    value_heads = value_rows.reshape(slot_count, local_heads, HD)
    grad_heads = grad_rows.reshape(slot_count, local_heads, HD)
    piece_keys = lax.all_gather(key_rows, "seq", axis=0, tiled=True)
    piece_values = lax.all_gather(value_rows, "seq", axis=0, tiled=True)
    piece_live = lax.all_gather(live_half, "seq", axis=0, tiled=True)
    running_max = jnp.full((local_heads, slot_count), masked_score, jnp.float32)
    piece_rows = piece_keys.shape[0]
    key_ids = jnp.arange(piece_rows, dtype=jnp.int32)
    allowed = (key_ids[None, :] <= own_ids[:, None]) & (piece_live[None, :] > 0.5)
    scores = (
        jnp.einsum(
            "qhd,khd->hqk",
            query_heads,
            piece_keys.reshape(piece_rows, local_heads, HD),
            preferred_element_type=jnp.float32,
        )
        * score_scale
    )
    scores = jnp.where(allowed[None], scores, masked_score)
    new_max = jnp.maximum(running_max, jnp.max(scores, axis=2))
    softmax_part = jnp.exp(scores - new_max[:, :, None])
    new_sum = jnp.sum(softmax_part, axis=2)
    product = jnp.einsum(
        "hqk,khd->hqd",
        softmax_part.astype(jnp.bfloat16),
        piece_values.reshape(piece_rows, local_heads, HD),
        preferred_element_type=jnp.float32,
    )
    attention = jnp.transpose(product / new_sum[:, :, None], (1, 0, 2)).reshape(
        slot_count, head_width
    )
    attended = jnp.where(live_mask[:, None], attention, jnp.float32(0.0)).astype(jnp.bfloat16)
    log_rows = jnp.transpose(new_max + jnp.log(new_sum))
    delta_rows = jnp.sum(
        grad_heads.astype(jnp.float32)
        * attended.reshape(slot_count, local_heads, HD).astype(jnp.float32),
        axis=2,
    )
    own_logs = jnp.transpose(log_rows)
    own_deltas = jnp.transpose(delta_rows)
    all_logs, all_deltas = (
        lax.all_gather(log_rows, "seq", axis=0, tiled=True),
        lax.all_gather(delta_rows, "seq", axis=0, tiled=True),
    )
    piece_queries = lax.all_gather(queries, "seq", axis=0, tiled=True)
    piece_keys = lax.all_gather(key_rows, "seq", axis=0, tiled=True)
    piece_values = lax.all_gather(value_rows, "seq", axis=0, tiled=True)
    piece_grads = lax.all_gather(grad_rows, "seq", axis=0, tiled=True)
    piece_live = lax.all_gather(live_half, "seq", axis=0, tiled=True)
    piece_rows = piece_keys.shape[0]
    key_ids = jnp.arange(piece_rows, dtype=jnp.int32)
    key_part = piece_keys.reshape(piece_rows, local_heads, HD)
    allowed = (key_ids[None, :] <= own_ids[:, None]) & (piece_live[None, :] > 0.5)
    scores = (
        jnp.einsum("qhd,khd->hqk", query_heads, key_part, preferred_element_type=jnp.float32)
        * score_scale
    )
    scores = jnp.where(allowed[None], scores, masked_score)
    probs_full = jnp.exp(scores - own_logs[:, :, None])
    grad_probs = jnp.einsum(
        "qhd,khd->hqk",
        grad_heads,
        piece_values.reshape(piece_rows, local_heads, HD),
        preferred_element_type=jnp.float32,
    )
    grad_scores = (probs_full * (grad_probs - own_deltas[:, :, None])).astype(jnp.bfloat16)
    new_query = jnp.einsum(
        "hqk,khd->hqd", grad_scores, key_part, preferred_element_type=jnp.float32
    )
    piece_rows = piece_queries.shape[0]
    piece_ids = jnp.arange(piece_rows, dtype=jnp.int32)
    query_part = piece_queries.reshape(piece_rows, local_heads, HD)
    grad_part = piece_grads.reshape(piece_rows, local_heads, HD)
    piece_logs = jnp.transpose(all_logs)
    piece_deltas = jnp.transpose(all_deltas)
    allowed = (own_ids[None, :] <= piece_ids[:, None]) & live_mask[None, :]
    scores = (
        jnp.einsum("qhd,khd->hqk", query_part, key_heads, preferred_element_type=jnp.float32)
        * score_scale
    )
    scores = jnp.where(allowed[None], scores, masked_score)
    probs_full = jnp.exp(scores - piece_logs[:, :, None])
    grad_value = jnp.einsum(
        "hqk,qhd->hkd",
        probs_full.astype(jnp.bfloat16),
        grad_part,
        preferred_element_type=jnp.float32,
    )
    grad_probs = jnp.einsum(
        "qhd,khd->hqk", grad_part, value_heads, preferred_element_type=jnp.float32
    )
    grad_scores = (probs_full * (grad_probs - piece_deltas[:, :, None])).astype(jnp.bfloat16)
    grad_key = jnp.einsum(
        "hqk,qhd->hkd", grad_scores, query_part, preferred_element_type=jnp.float32
    )

    def to_rows(stacked):
        return jnp.transpose(stacked, (1, 0, 2)).reshape(slot_count, head_width)

    contract = (((1,), (1,)), ((), ()))
    query_grad_rows = (to_rows(new_query) * score_scale).astype(jnp.bfloat16)
    key_grad_rows = (to_rows(grad_key) * score_scale).astype(jnp.bfloat16)
    value_grad_rows = to_rows(grad_value).astype(jnp.bfloat16)
    partial_normed = lax.dot_general(
        query_grad_rows, query_weight, contract, preferred_element_type=jnp.float32
    )
    partial_normed = partial_normed + lax.dot_general(
        key_grad_rows, key_weight, contract, preferred_element_type=jnp.float32
    )
    partial_normed = partial_normed + lax.dot_general(
        value_grad_rows, value_weight, contract, preferred_element_type=jnp.float32
    )
    grad_normed = lax.psum(partial_normed.astype(jnp.bfloat16), "head").astype(jnp.float32)
    scaled_grad = norm_gain * grad_normed
    cubed = inverse_rms * inverse_rms * inverse_rms
    grad_state = (
        inverse_rms[:, None] * scaled_grad
        - span_state * cubed[:, None] * jnp.mean(scaled_grad * span_state, axis=1)[:, None]
    )
    grad_state = jnp.where(live_mask[:, None], grad_state, jnp.float32(0.0))
    mixed_grad = lax.dot_general(
        grad_state.astype(jnp.bfloat16), mix_weight, contract, preferred_element_type=jnp.float32
    )
    spread_mix = jnp.zeros((row_count, D), jnp.float32).at[boundaries].add(mixed_grad)
    residual_grad = jnp.zeros((row_count, D), jnp.float32).at[boundaries].add(grad_state)
    after_rim = neighbour(spread_mix[: KCONV - 1], -1)
    padded_grad = jnp.concatenate([spread_mix, after_rim], axis=0)
    conv_grad = conv_kernel[0] * spread_mix
    for offset in range(1, KCONV):
        conv_grad = conv_grad + conv_kernel[offset] * padded_grad[offset : offset + row_count]
    grad_bytes = (residual_grad + conv_grad).astype(jnp.bfloat16)
    return (attended, grad_bytes)


def solution(mesh):
    return jax.shard_map(
        per_device,
        mesh=mesh,
        in_specs=(
            P(("doc", "seq"), None),
            P(),
            P(),
            P(),
            P(None, "head"),
            P(None, "head"),
            P(None, "head"),
            P(("doc", "seq")),
            P(("doc", "seq")),
            P(("doc", "seq"), "head"),
        ),
        out_specs=(P(("doc", "seq"), "head"), P(("doc", "seq"), None)),
        check_vma=False,
    )
```

profile of v0, /device:TPU:56, one launch (start us, length us, event | category | flops | bytes accessed | tf_op | source)
XLA Modules:
  0.0 557.7 jit_solution(17123047837741712854)
XLA Ops:
  7.2 0.0 copy-start
  7.2 0.0 all-reduce.6.cloned.1.call-start
  7.2 0.9 slice.68
  8.1 2.6 collective-permute-start
  10.7 0.7 compare_select_fusion.1
  11.4 1.3 compare_and_fusion.4
  13.3 0.5 iota_add_fusion
  13.8 1.3 dynamic-slice
  15.8 0.2 dynamic-update-slice
  16.0 63.5 %all-reduce = bf16[2048]{0:T(1024)(128)(2,1)S(1)} all-reduce(bf16[2048]{0:T(1024)(128)(2,1)S(1)} %dynamic-update-slice), channel_id=1, replica_groups=mesh['seq'=32,'head'=8,'doc'=2] {'seq'}, use_global_device_ids=true, to_apply=%add | all-reduce | flops 2048 | bytes 8192
  79.5 0.6 broadcast_compare_fusion
  80.1 1.5 fusion.54
  81.6 0.0 copy-done.15
  81.6 0.5 iota_compare_fusion.2
  82.1 2.2 gather_fusion
  84.3 0.0 collective-permute-done
  84.3 1.5 pad_maximum_fusion
  85.8 1.4 gather_fusion.4
  87.2 1.4 gather_fusion.3
  88.5 1.3 gather_fusion.2
  89.9 1.4 gather_fusion.1
  91.2 0.0 copy-done
  91.2 1.9 multiply_reduce_fusion.1
  93.2 0.0 copy-start.12
  93.2 0.0 copy-start.14
  93.2 0.0 copy-done.9
  93.2 0.1 multiply_convert_fusion
  93.3 0.0 copy-done.8
  93.3 0.2 convolution_convert_fusion.1
  93.5 0.0 copy-done.6
  93.5 0.0 copy-start.11
  93.5 0.0 copy-start.13
  93.5 0.2 convolution_convert_fusion.2
  93.7 0.2 convolution_convert_fusion.3
  93.9 60.8 %all_gather.27 = bf16[2048,128]{1,0:T(8,128)(2,1)} all-gather(bf16[64,128]{1,0:T(8,128)(2,1)S(1)} %convolution_convert_fusion.3), channel_id=1, replica_groups=mesh['seq'=32,'head'=8,'doc'=2] {'seq'}, dimensions={0}, use_global_device_ids=true | all-gather | bytes 540672 | tf_op jit(solution)/shard_map/all_gather | solution.py:110
  154.7 48.0 %all_gather.25 = bf16[2048,128]{1,0:T(8,128)(2,1)S(1)} all-gather(bf16[64,128]{1,0:T(8,128)(2,1)S(1)} %convolution_convert_fusion.2), channel_id=1, replica_groups=mesh['seq'=32,'head'=8,'doc'=2] {'seq'}, dimensions={0}, use_global_device_ids=true | all-gather | bytes 540672 | tf_op jit(solution)/shard_map/all_gather | solution.py:68
  202.7 0.0 copy-start.2
  202.7 0.4 fusion.55
  203.1 47.6 %all_gather.26 = bf16[2048,128]{1,0:T(8,128)(2,1)S(1)} all-gather(bf16[64,128]{1,0:T(8,128)(2,1)S(1)} %convolution_convert_fusion.1), channel_id=1, replica_groups=mesh['seq'=32,'head'=8,'doc'=2] {'seq'}, dimensions={0}, use_global_device_ids=true | all-gather | bytes 540672 | tf_op jit(solution)/shard_map/all_gather | solution.py:69
  250.8 0.2 fusion.26
  251.0 0.1 fusion.53
  251.1 1.0 multiply_reduce_fusion.2
  252.2 48.0 %all_gather.29 = bf16[2048,128]{1,0:T(8,128)(2,1)S(1)} all-gather(bf16[64,128]{1,0:T(8,128)(2,1)S(1)} %get-tuple-element.8), channel_id=1, replica_groups=mesh['seq'=32,'head'=8,'doc'=2] {'seq'}, dimensions={0}, use_global_device_ids=true | all-gather | bytes 540672 | tf_op jit(solution)/shard_map/all_gather | solution.py:113
  300.2 1.7 fusion.19
  301.8 0.0 copy-start.4
  301.8 0.3 dynamic-update-slice.2
  302.1 1.8 fusion.56
  304.0 126.1 %all-reduce.3 = (f32[2048]{0:T(1024)S(1)}, f32[2048]{0:T(1024)S(1)}) all-reduce(f32[2048]{0:T(1024)S(1)} %get-tuple-element.5, f32[2048]{0:T(1024)S(1)} %dynamic-update-slice.2), channel_id=2, replica_groups=mesh['seq'=32,'head'=8,'doc'=2] {'seq'}, use_global_device_ids=true, to_apply=%add.1 | all-reduce | flops 4096 | bytes 32768
  430.1 2.2 fusion.5
  432.3 1.5 fusion.18
  433.7 1.2 convolution_add_fusion.1
  435.0 2.1 fusion.13
  437.1 0.0 all-reduce.6.cloned.1.call-update
  437.2 90.4 %all-reduce.6.cloned.1.call-done = bf16[64,1024]{1,0:T(8,128)(2,1)} async-done(((bf16[64,1024]{1,0:T(8,128)(2,1)}), bf16[64,1024]{1,0:T(8,128)(2,1)}) %all-reduce.6.cloned.1.call-update) | async-done | bytes 131088 | tf_op jit(solution)/shard_map/psum | solution.py:178
  527.6 1.0 multiply_reduce_fusion
  528.7 1.7 fusion.39
  530.3 2.6 scatter_custom_fusion
  533.0 0.8 slice.50
  533.7 3.5 collective-permute-start.1
  537.2 1.8 constant_dynamic-update-slice_fusion.1
  539.1 2.5 collective-permute-done.1
  541.6 2.2 fusion.8
  543.9 4.2 scatter_custom_fusion.1
  548.1 2.7 convert_element_type.113
  (31 shorter events, 0.1 us)
Async XLA Ops:
  7.2 84.1 %copy-start = (bf16[1024,1024]{1,0:T(8,128)(2,1)S(1)}, bf16[1024,1024]{1,0:T(8,128)(2,1)}, u32[]{:S(2)}) copy-start(bf16[1024,1024]{1,0:T(8,128)(2,1)} %param.14) | copy-start | bytes 6291460
  7.2 520.4 %all-reduce.6.cloned.1.call-start = ((), (), s32[]{:S(2)}) async-start(), calls=%async_computation | async-start | bytes 262144 | tf_op jit(solution)/shard_map/psum | solution.py:178
  8.1 76.2 %collective-permute-start = (bf16[3,1024]{1,0:T(4,128)(2,1)S(1)}, bf16[3,1024]{1,0:T(4,128)(2,1)S(1)}, u32[]{:S(2)}, u32[]{:S(2)}) collective-permute-start(bf16[3,1024]{1,0:T(4,128)(2,1)S(1)} %slice.68), channel_id=1, source_target_pairs={{0,16},{16,32},{32,48},{48,64},{64,80},{80,96},{96,112},{112,128},... | collective-permute-start | bytes 18440 | tf_op jit(solution)/shard_map/ppermute | solution.py:16
  11.4 70.2 %copy-start.15 = (s32[64]{0:T(128)}, s32[64]{0:T(128)S(1)}, u32[]{:S(2)}) copy-start(s32[64]{0:T(128)S(1)} %get-tuple-element.29) | copy-start | bytes 772
  89.9 3.4 copy-start.9
  91.2 2.1 copy-start.8
  91.2 2.3 copy-start.6
  91.2 2.5 copy-start.7
  93.2 109.5 %copy-start.12 = (pred[2048]{0:T(1024)(128)(4,1)S(1)}, pred[2048]{0:T(1024)(128)(4,1)}, u32[]{:S(2)}) copy-start(pred[2048]{0:T(1024)(128)(4,1)} %broadcast_compare_fusion) | copy-start | bytes 6148
  93.2 109.5 %copy-start.14 = (s32[64]{0:T(128)S(1)}, s32[64]{0:T(128)}, u32[]{:S(2)}) copy-start(s32[64]{0:T(128)} %iota_add_fusion) | copy-start | bytes 772
  93.5 157.6 %copy-start.11 = (bf16[64,128]{1,0:T(8,128)(2,1)S(1)}, bf16[64,128]{1,0:T(8,128)(2,1)}, u32[]{:S(2)}) copy-start(bf16[64,128]{1,0:T(8,128)(2,1)} %param.21) | copy-start | bytes 49156
  93.5 157.6 %copy-start.13 = (pred[64]{0:T(512)(128)(4,1)S(1)}, pred[64]{0:T(512)(128)(4,1)}, u32[]{:S(2)}) copy-start(pred[64]{0:T(512)(128)(4,1)} %iota_compare_fusion.2) | copy-start | bytes 196
  202.7 49.4 %copy-start.2 = (bf16[2048,128]{1,0:T(8,128)(2,1)}, bf16[2048,128]{1,0:T(8,128)(2,1)S(1)}, u32[]{:S(2)}) copy-start(bf16[2048,128]{1,0:T(8,128)(2,1)S(1)} %all_gather.25) | copy-start | bytes 1572868
  250.7 1.4 copy-start.3
  301.8 130.4 %copy-start.4 = (bf16[2048,128]{1,0:T(8,128)(2,1)S(1)}, bf16[2048,128]{1,0:T(8,128)(2,1)}, u32[]{:S(2)}) copy-start(bf16[2048,128]{1,0:T(8,128)(2,1)} %all_gather.27) | copy-start | bytes 1572868
  533.7 7.9 %copy-start.1 = (f32[512,1024]{1,0:T(8,128)S(1)}, f32[512,1024]{1,0:T(8,128)}, u32[]{:S(2)}) copy-start(f32[512,1024]{1,0:T(8,128)} %scatter_custom_fusion) | copy-start | bytes 6291460
  533.7 7.9 %copy-start.10 = (f32[1,1024]{1,0:T(1,128)S(1)}, f32[1,1024]{1,0:T(1,128)}, u32[]{:S(2)}) copy-start(f32[1,1024]{1,0:T(1,128)} %get-tuple-element.18) | copy-start | bytes 12292
  533.7 7.9 %collective-permute-start.1 = (f32[3,1024]{1,0:T(4,128)S(1)}, f32[3,1024]{1,0:T(4,128)S(1)}, u32[]{:S(2)}, u32[]{:S(2)}) collective-permute-start(f32[3,1024]{1,0:T(4,128)S(1)} %slice.50), channel_id=1, source_target_pairs={{16,0},{32,16},{48,32},{64,48},{80,64},{96,80},{112,96},{128,112},... | collective-permute-start | bytes 36872 | tf_op jit(solution)/shard_map/ppermute | solution.py:16
  541.6 2.2 copy-start.5
Sparse Core Ops, SparseCore 0:
  437.3 90.2 all-reduce.5
where the time goes:
time: 559 us; the launch traced here: 558 us
  blocking collectives  394 us (70%)
  waiting for transfers between devices  93 us (17%)
  other arithmetic  18.4 us (3%)
  matrix products  16.1 us (3%)
  between operations  15.6 us (3%)
  local copies, waits for them, and re-layouts  14.4 us (3%)
  starting transfers between devices  6.1 us (1%)
    unnamed x2, blocking collectives  190 us
    psum x1, waiting for transfers between devices, per_device(): lax.psum(partial_normed.astype(jnp.bfloat16), 'head').astype(jnp.float32)  90.4 us
    all_gather x1, blocking collectives, per_device(): piece_queries = lax.all_gather(queries, 'seq', axis=0, tiled=True)  60.8 us
    all_gather x1, blocking collectives, per_device(): piece_grads = lax.all_gather(grad_rows, 'seq', axis=0, tiled=True)  48 us
    all_gather x1, blocking collectives, per_device(): piece_keys = lax.all_gather(key_rows, 'seq', axis=0, tiled=True)  48 us
    all_gather x1, blocking collectives, per_device(): piece_values = lax.all_gather(value_rows, 'seq', axis=0, tiled=True)  47.6 us
  transfers between devices with their start and end apart: 3, of which 2 were waited for; matrix products, arithmetic and copies ran while one was open for 2% of the time, Pallas kernels for 0%

commit v1 on v0

--- a/solution.py
+++ b/solution.py
@@ -110,7 +110,9 @@
     piece_queries = lax.all_gather(queries, "seq", axis=0, tiled=True)
     piece_keys = lax.all_gather(key_rows, "seq", axis=0, tiled=True)
     piece_values = lax.all_gather(value_rows, "seq", axis=0, tiled=True)
-    piece_grads = lax.all_gather(grad_rows, "seq", axis=0, tiled=True)
+    piece_grads = jnp.concatenate(
+        lax.all_to_all(jnp.stack([grad_rows] * lax.axis_size("seq")), "seq", 0, 0), axis=0
+    )
     piece_live = lax.all_gather(live_half, "seq", axis=0, tiled=True)
     piece_rows = piece_keys.shape[0]
     key_ids = jnp.arange(piece_rows, dtype=jnp.int32)

time: 559 us -> 523 us (0.936)
  blocking collectives: 394 us -> 362 us
  waiting for transfers between devices: 93 us -> 80.4 us
  starting transfers between devices: 6.1 us -> 12.8 us
    all_gather x1 -> x0, blocking collectives: 48 us -> none  [per_device(): piece_grads = lax.all_gather(grad_rows, 'seq', axis=0, tiled=True)]
    psum x1, waiting for transfers between devices: 90.4 us -> 77.8 us  [per_device(): lax.psum(partial_normed.astype(jnp.bfloat16), 'head').astype(jnp.float32)]
    all_gather x1, blocking collectives: 48 us -> 56.4 us  [per_device(): piece_keys = lax.all_gather(key_rows, 'seq', axis=0, tiled=True)]
    all_to_all x0 -> x1, starting transfers between devices: none -> 6.66 us  [per_device(): lax.all_to_all(jnp.stack([grad_rows] * lax.axis_size('seq')), 'seq', 0, 0)]
  transfers between devices with their start and end apart: 3 -> 4, of which waited for: 2 -> 2; matrix products, arithmetic and copies ran while one was open for 2% -> 3% of each run, Pallas kernels for 0% -> 0%
where the time goes in v1:
time: 523 us; the launch traced here: 522 us
  blocking collectives  362 us (69%)
  waiting for transfers between devices  80.4 us (15%)
  other arithmetic  18.4 us (4%)
  local copies, waits for them, and re-layouts  16.6 us (3%)
  matrix products  16.1 us (3%)
  between operations  15.6 us (3%)
  starting transfers between devices  12.8 us (2%)
    unnamed x2, blocking collectives  191 us
    psum x1, waiting for transfers between devices, per_device(): lax.psum(partial_normed.astype(jnp.bfloat16), 'head').astype(jnp.float32)  77.8 us
    all_gather x1, blocking collectives, per_device(): piece_queries = lax.all_gather(queries, 'seq', axis=0, tiled=True)  66.1 us
    all_gather x1, blocking collectives, per_device(): piece_keys = lax.all_gather(key_rows, 'seq', axis=0, tiled=True)  56.4 us
    all_gather x1, blocking collectives, per_device(): piece_values = lax.all_gather(value_rows, 'seq', axis=0, tiled=True)  48.4 us
  transfers between devices with their start and end apart: 4, of which 2 were waited for; matrix products, arithmetic and copies ran while one was open for 3% of the time, Pallas kernels for 0%

profile of v1, /device:TPU:56, one launch (start us, length us, event | category | flops | bytes accessed | tf_op | source)
XLA Modules:
  0.0 522.0 jit_solution(2005950302565231299)
XLA Ops:
  7.2 0.0 copy-start
  7.2 0.9 slice.68
  8.1 2.6 collective-permute-start
  10.7 0.7 compare_select_fusion.1
  11.3 1.2 compare_and_fusion.4
  13.2 0.5 iota_add_fusion
  13.7 1.3 dynamic-slice
  15.7 0.2 dynamic-update-slice
  15.9 63.5 %all-reduce = bf16[2048]{0:T(1024)(128)(2,1)S(1)} all-reduce(bf16[2048]{0:T(1024)(128)(2,1)S(1)} %dynamic-update-slice), channel_id=1, replica_groups=mesh['seq'=32,'head'=8,'doc'=2] {'seq'}, use_global_device_ids=true, to_apply=%add | all-reduce | flops 2048 | bytes 8192
  79.5 0.6 broadcast_compare_fusion
  80.0 1.5 fusion.54
  81.5 0.0 copy-done.16
  81.5 0.5 iota_compare_fusion.2
  82.1 2.2 gather_fusion
  84.2 0.0 collective-permute-done
  84.3 1.5 pad_maximum_fusion
  85.8 1.4 gather_fusion.4
  87.1 1.3 gather_fusion.3
  88.5 1.4 gather_fusion.2
  89.8 1.3 gather_fusion.1
  91.2 0.0 copy-start.12
  91.2 0.0 copy-start.14
  91.2 1.9 multiply_reduce_fusion.1
  93.2 0.0 copy-start.11
  93.2 0.1 multiply_convert_fusion
  93.3 0.2 convolution_convert_fusion.1
  93.5 0.0 copy-done.6
  93.5 0.2 convolution_convert_fusion.2
  93.7 0.2 convolution_convert_fusion.3
  93.9 56.4 %all_gather.22 = bf16[2048,128]{1,0:T(8,128)(2,1)S(1)} all-gather(bf16[64,128]{1,0:T(8,128)(2,1)S(1)} %convolution_convert_fusion.2), channel_id=1, replica_groups=mesh['seq'=32,'head'=8,'doc'=2] {'seq'}, dimensions={0}, use_global_device_ids=true | all-gather | bytes 540672 | tf_op jit(solution)/shard_map/all_gather | solution.py:68
  150.2 0.8 copy-done.2
  151.0 0.0 copy-done.12
  151.0 0.4 fusion.55
  151.5 48.4 %all_gather.23 = bf16[2048,128]{1,0:T(8,128)(2,1)S(1)} all-gather(bf16[64,128]{1,0:T(8,128)(2,1)S(1)} %convolution_convert_fusion.1), channel_id=1, replica_groups=mesh['seq'=32,'head'=8,'doc'=2] {'seq'}, dimensions={0}, use_global_device_ids=true | all-gather | bytes 540672 | tf_op jit(solution)/shard_map/all_gather | solution.py:69
  199.9 0.2 fusion.26
  200.1 0.5 copy-done.3
  200.7 1.0 multiply_reduce_fusion.2
  201.7 0.9 stack.2
  202.6 6.7 %all-to-all-start = ((bf16[32,64,128]{2,1,0:T(8,128)(2,1)}), bf16[32,64,128]{2,1,0:T(8,128)(2,1)S(1)}, u32[]{:S(2)}, u32[]{:S(2)}) async-start(bf16[32,64,128]{2,1,0:T(8,128)(2,1)} %stack.2), calls=%async_computation | async-start | bytes 1048576 | tf_op jit(solution)/shard_map/all_to_all | solution.py:114
  209.3 0.0 all-reduce.6.cloned.1.call-start
  209.3 0.3 dynamic-update-slice.2
  209.6 0.1 fusion.53
  209.7 127.6 %all-reduce.3 = (f32[2048]{0:T(1024)S(1)}, f32[2048]{0:T(1024)S(1)}) all-reduce(f32[2048]{0:T(1024)S(1)} %get-tuple-element.5, f32[2048]{0:T(1024)S(1)} %dynamic-update-slice.2), channel_id=2, replica_groups=mesh['seq'=32,'head'=8,'doc'=2] {'seq'}, use_global_device_ids=true, to_apply=%add.1 | all-reduce | flops 4096 | bytes 32768
  337.4 66.1 %all_gather.24 = bf16[2048,128]{1,0:T(8,128)(2,1)} all-gather(bf16[64,128]{1,0:T(8,128)(2,1)S(1)} %convolution_convert_fusion.3), channel_id=1, replica_groups=mesh['seq'=32,'head'=8,'doc'=2] {'seq'}, dimensions={0}, use_global_device_ids=true | all-gather | bytes 540672 | tf_op jit(solution)/shard_map/all_gather | solution.py:110
  403.4 1.7 fusion.19
  405.1 1.9 fusion.56
  407.0 2.2 fusion.5
  409.2 0.0 all-to-all-done
  409.2 1.5 fusion.18
  410.7 1.2 convolution_add_fusion.1
  411.9 2.1 fusion.13
  414.1 0.0 all-reduce.6.cloned.1.call-update
  414.1 77.8 %all-reduce.6.cloned.1.call-done = bf16[64,1024]{1,0:T(8,128)(2,1)} async-done(((bf16[64,1024]{1,0:T(8,128)(2,1)}), bf16[64,1024]{1,0:T(8,128)(2,1)}) %all-reduce.6.cloned.1.call-update) | async-done | bytes 131088 | tf_op jit(solution)/shard_map/psum | solution.py:180
  491.9 1.0 multiply_reduce_fusion
  493.0 1.7 fusion.39
  494.7 2.7 scatter_custom_fusion
  497.3 0.8 slice.50
  498.1 3.5 collective-permute-start.1
  501.6 1.8 constant_dynamic-update-slice_fusion.1
  503.4 2.6 collective-permute-done.1
  506.0 2.2 fusion.8
  508.2 0.0 copy-done.5
  508.2 4.2 scatter_custom_fusion.1
  512.5 2.7 convert_element_type.113
  (35 shorter events, 0.1 us)
Async XLA Ops:
  7.2 84.0 %copy-start = (bf16[1024,1024]{1,0:T(8,128)(2,1)S(1)}, bf16[1024,1024]{1,0:T(8,128)(2,1)}, u32[]{:S(2)}) copy-start(bf16[1024,1024]{1,0:T(8,128)(2,1)} %param.14) | copy-start | bytes 6291460
  8.1 76.2 %collective-permute-start = (bf16[3,1024]{1,0:T(4,128)(2,1)S(1)}, bf16[3,1024]{1,0:T(4,128)(2,1)S(1)}, u32[]{:S(2)}, u32[]{:S(2)}) collective-permute-start(bf16[3,1024]{1,0:T(4,128)(2,1)S(1)} %slice.68), channel_id=1, source_target_pairs={{0,16},{16,32},{32,48},{48,64},{64,80},{80,96},{96,112},{112,128},... | collective-permute-start | bytes 18440 | tf_op jit(solution)/shard_map/ppermute | solution.py:16
  11.3 70.2 %copy-start.16 = (s32[64]{0:T(128)}, s32[64]{0:T(128)S(1)}, u32[]{:S(2)}) copy-start(s32[64]{0:T(128)S(1)} %get-tuple-element.29) | copy-start | bytes 772
  89.8 3.3 copy-start.9
  91.2 2.1 copy-start.8
  91.2 2.3 copy-start.6
  91.2 2.5 copy-start.7
  91.2 59.8 %copy-start.12 = (pred[2048]{0:T(1024)(128)(4,1)S(1)}, pred[2048]{0:T(1024)(128)(4,1)}, u32[]{:S(2)}) copy-start(pred[2048]{0:T(1024)(128)(4,1)} %broadcast_compare_fusion) | copy-start | bytes 6148
  91.2 59.8 %copy-start.14 = (s32[64]{0:T(128)S(1)}, s32[64]{0:T(128)}, u32[]{:S(2)}) copy-start(s32[64]{0:T(128)} %iota_add_fusion) | copy-start | bytes 772
  93.2 107.5 %copy-start.11 = (bf16[64,128]{1,0:T(8,128)(2,1)S(1)}, bf16[64,128]{1,0:T(8,128)(2,1)}, u32[]{:S(2)}) copy-start(bf16[64,128]{1,0:T(8,128)(2,1)} %param.21) | copy-start | bytes 49156
  93.2 107.5 %copy-start.13 = (pred[64]{0:T(512)(128)(4,1)S(1)}, pred[64]{0:T(512)(128)(4,1)}, u32[]{:S(2)}) copy-start(pred[64]{0:T(512)(128)(4,1)} %iota_compare_fusion.2) | copy-start | bytes 196
  150.2 0.8 copy-start.2
  199.9 0.8 copy-start.3
  201.7 205.3 %copy-start.15 = (s32[64]{0:T(128)S(1)}, s32[64]{0:T(128)}, u32[]{:S(2)}) copy-start(s32[64]{0:T(128)} %iota_add_fusion) | copy-start | bytes 772
  202.6 206.6 %all-to-all-start = ((bf16[32,64,128]{2,1,0:T(8,128)(2,1)}), bf16[32,64,128]{2,1,0:T(8,128)(2,1)S(1)}, u32[]{:S(2)}, u32[]{:S(2)}) async-start(bf16[32,64,128]{2,1,0:T(8,128)(2,1)} %stack.2), calls=%async_computation | async-start | bytes 1048576 | tf_op jit(solution)/shard_map/all_to_all | solution.py:114
  209.3 282.7 %all-reduce.6.cloned.1.call-start = ((), (), s32[]{:S(2)}) async-start(), calls=%async_computation.1 | async-start | bytes 262144 | tf_op jit(solution)/shard_map/psum | solution.py:180
  405.1 4.1 copy-start.4
  498.1 7.9 %copy-start.1 = (f32[512,1024]{1,0:T(8,128)S(1)}, f32[512,1024]{1,0:T(8,128)}, u32[]{:S(2)}) copy-start(f32[512,1024]{1,0:T(8,128)} %scatter_custom_fusion) | copy-start | bytes 6291460
  498.1 7.9 %copy-start.10 = (f32[1,1024]{1,0:T(1,128)S(1)}, f32[1,1024]{1,0:T(1,128)}, u32[]{:S(2)}) copy-start(f32[1,1024]{1,0:T(1,128)} %get-tuple-element.18) | copy-start | bytes 12292
  498.1 7.9 %collective-permute-start.1 = (f32[3,1024]{1,0:T(4,128)S(1)}, f32[3,1024]{1,0:T(4,128)S(1)}, u32[]{:S(2)}, u32[]{:S(2)}) collective-permute-start(f32[3,1024]{1,0:T(4,128)S(1)} %slice.50), channel_id=1, source_target_pairs={{16,0},{32,16},{48,32},{64,48},{80,64},{96,80},{112,96},{128,112},... | collective-permute-start | bytes 36872 | tf_op jit(solution)/shard_map/ppermute | solution.py:16
  506.0 2.2 copy-start.5
Sparse Core Ops, SparseCore 0:
  414.2 77.6 all-reduce.5
